TPU v7x, 32 devices: a whole 2x2x4 slice. The times are simulated.
32 devices in a mesh: row: 8 (over y, x, core), col: 4 (over z).
Axes of the slice: x: 2, y: 2, z: 4, core: 2. Of those that a mesh axis runs over, the one named last changes fastest.
Arguments:
- pair_rep: bfloat16 [128, 128, 128], P(('row', 'col')), may hold values from -16 to 16
- tile_mask: int32 [1, 1], replicated, may hold values from 0 to 1, as said below
- chain_ids: int32 [128], replicated, may hold values from 0 to 3, never falling along the last dimension, each value on 1 to 64 neighbouring positions
- chain_bias: float32 [2, 4], replicated, may hold values from -6 to 6
- row_project: bfloat16 [128, 512], replicated, may hold values from -0.5 to 0.5
- row_bias_proj: bfloat16 [128, 4], replicated, may hold values from -36 to 36
- row_output: bfloat16 [128, 128], replicated, may hold values from -0.5 to 0.5
- col_project: bfloat16 [128, 512], replicated, may hold values from -0.5 to 0.5
- col_bias_proj: bfloat16 [128, 4], replicated, may hold values from -36 to 36
- col_output: bfloat16 [128, 128], replicated, may hold values from -0.5 to 0.5
- tri_left: bfloat16 [128, 256], replicated, may hold values from -0.5 to 0.5
- tri_right: bfloat16 [128, 256], replicated, may hold values from -0.5 to 0.5
- tri_gate: bfloat16 [128, 128], replicated, may hold values from -0.5 to 0.5
- tri_output: bfloat16 [128, 128], replicated, may hold values from -1.5 to 1.5
Outputs:
- pair_out: bfloat16 [128, 128, 128], P('row', 'col')
Inputs may be any that keep to these rules, and one draw needn't show every extreme that they name: `tile_mask`: every diagonal entry is 1. `chain_ids`: chain numbers never fall along the residues.
All inputs are finite; a program needn't handle non-finite values.
Results may differ from a plain program's by a relative error of at most 0.018.
Values may be sent and summed in bfloat16 or wider, within the bound.
No kernel may reach another device: no remote copies, remote signals or barrier semaphores. Data moves between devices by JAX's collectives and lax.ppermute only.
A program may use at most 64 MiB of HBM per device.

v0:
```python
import jax
import jax.numpy as jnp
from jax import lax
from jax.sharding import PartitionSpec as P


def layer_norm(values):
    values = values.astype(jnp.float32)
    center = values - jnp.mean(values, axis=-1, keepdims=True)
    spread = jnp.mean(center * center, axis=-1, keepdims=True)
    return center * lax.rsqrt(spread + 1e-05)


def tile_rows(positions, tile_table, length):
    tile_count = tile_table.shape[0]
    tile_width = length // tile_count
    onehot = (positions[:, None] // tile_width == jnp.arange(tile_count)[None, :]).astype(
        jnp.float32
    )
    picked = jnp.dot(onehot, tile_table.astype(jnp.float32))
    spread_out = jnp.broadcast_to(picked[:, :, None], (positions.shape[0], tile_count, tile_width))
    return spread_out.reshape(positions.shape[0], length) > 0.5


def tile_pairs(row_pos, col_pos, tile_table, length):
    tile_count = tile_table.shape[0]
    tile_width = length // tile_count
    row_hot = (row_pos[:, None] // tile_width == jnp.arange(tile_count)[None, :]).astype(
        jnp.float32
    )
    col_hot = (col_pos[:, None] // tile_width == jnp.arange(tile_count)[None, :]).astype(
        jnp.float32
    )
    return jnp.dot(jnp.dot(row_hot, tile_table.astype(jnp.float32)), col_hot.T)


def attend_lines(
    queries,
    key_rows,
    value_rows,
    gate_pre,
    bias_all,
    key_ok,
    chain_ids,
    chain_add,
    line_dim,
    flipped,
):
    line_count = queries.shape[line_dim]
    length = queries.shape[1 - line_dim]
    head_count = queries.shape[2]
    head_size = queries.shape[3]
    width_all = head_count * head_size
    query_rows = min(128, length)
    per_line = length // query_rows
    scaling = head_size ** (-0.5)

    def one_block(block_index):
        line_index = block_index // per_line
        offset = block_index % per_line * query_rows
        query_line = lax.dynamic_index_in_dim(queries, line_index, line_dim, keepdims=False)
        query_block = lax.dynamic_slice_in_dim(query_line, offset, query_rows, 0)
        key_line = lax.dynamic_index_in_dim(key_rows, line_index, line_dim, keepdims=False)
        value_line = lax.dynamic_index_in_dim(value_rows, line_index, line_dim, keepdims=False)
        scores = (
            jnp.einsum("qhd,khd->hqk", query_block, key_line, preferred_element_type=jnp.float32)
            * scaling
        )
        if flipped:
            bias_block = lax.dynamic_slice_in_dim(bias_all, offset, query_rows, 2).transpose(
                0, 2, 1
            )
        else:
            bias_block = lax.dynamic_slice_in_dim(bias_all, offset, query_rows, 1)
        scores = scores + bias_block
        chain_block = lax.dynamic_slice_in_dim(chain_ids, offset, query_rows, 0)
        same_chain = (chain_block[:, None] == chain_ids[None, :]).astype(jnp.float32)
        scores = scores + chain_add[:, None, None] * same_chain[None]
        usable = lax.dynamic_index_in_dim(key_ok, line_index, 0, keepdims=False)
        scores = jnp.where(usable[None, None, :], scores, -1000000000.0)
        row_peak = jnp.max(scores, axis=-1, keepdims=True)
        weights = jnp.exp(scores - row_peak)
        attention = (weights / jnp.sum(weights, axis=-1, keepdims=True)).astype(jnp.bfloat16)
        mixed_rows = jnp.einsum(
            "hqk,khd->qhd", attention, value_line, preferred_element_type=jnp.float32
        ).reshape(query_rows, width_all)
        gate_line = lax.dynamic_index_in_dim(gate_pre, line_index, line_dim, keepdims=False)
        gate_block = lax.dynamic_slice_in_dim(gate_line, offset, query_rows, 0)
        return (mixed_rows * jax.nn.sigmoid(gate_block)).astype(jnp.bfloat16)

    outputs = lax.map(one_block, jnp.arange(line_count * per_line, dtype=jnp.int32))
    outputs = outputs.reshape(line_count, length, width_all)
    if line_dim == 1:
        outputs = outputs.transpose(1, 0, 2)
    return outputs


def tri_acts(normed, weights, allowed):
    channels = normed.shape[-1]
    projected = jnp.dot(normed.reshape(-1, channels), weights, preferred_element_type=jnp.float32)
    projected = projected.reshape(normed.shape[0], normed.shape[1], 2 * channels)
    return (
        jax.nn.sigmoid(projected[..., channels:]) * projected[..., :channels] * allowed[..., None]
    ).astype(jnp.bfloat16)


def shards(
    pair_rep,
    tile_mask,
    chain_ids,
    chain_bias,
    row_project,
    row_bias_proj,
    row_output,
    col_project,
    col_bias_proj,
    col_output,
    tri_left,
    tri_right,
    tri_gate,
    tri_output,
):
    n_row = lax.axis_size("row")
    n_col = lax.axis_size("col")
    device_count = n_row * n_col
    rows_here, length, channels = pair_rep.shape
    head_count = row_bias_proj.shape[1]
    head_size = channels // head_count
    row_index = lax.axis_index("row")
    col_index = lax.axis_index("col")
    device_index = row_index * n_col + col_index
    local_lines = device_index * rows_here + jnp.arange(rows_here, dtype=jnp.int32)
    normed = layer_norm(pair_rep).astype(jnp.bfloat16)
    flat_rows = normed.reshape(rows_here * length, channels)
    bias_rows = jnp.dot(flat_rows, row_bias_proj, preferred_element_type=jnp.float32)
    bias_rows = bias_rows.reshape(rows_here, length, head_count).transpose(2, 0, 1)
    bias_all = lax.all_gather(bias_rows, ("row", "col"), axis=1, tiled=True)
    projected = jnp.dot(flat_rows, row_project, preferred_element_type=jnp.float32).reshape(
        rows_here, length, 4 * channels
    )
    qkv_rows = (
        projected[..., : 3 * channels]
        .astype(jnp.bfloat16)
        .reshape(rows_here, length, 3, head_count, head_size)
    )
    key_ok = tile_rows(local_lines, tile_mask, length)
    mixed_rows = attend_lines(
        qkv_rows[:, :, 0],
        qkv_rows[:, :, 1],
        qkv_rows[:, :, 2],
        projected[..., 3 * channels :],
        bias_all,
        key_ok,
        chain_ids,
        chain_bias[0],
        0,
        False,
    )
    update = jnp.dot(
        mixed_rows.reshape(-1, channels), row_output, preferred_element_type=jnp.float32
    ).reshape(rows_here, length, channels)
    first_pair = (pair_rep.astype(jnp.float32) + update).astype(jnp.bfloat16)
    normed_first = layer_norm(first_pair).astype(jnp.bfloat16)
    bias_next = jnp.dot(
        normed_first.reshape(-1, channels), col_bias_proj, preferred_element_type=jnp.float32
    )
    bias_next = bias_next.reshape(rows_here, length, head_count).transpose(2, 0, 1)
    bias_cols = lax.all_gather(bias_next, ("row", "col"), axis=1, tiled=True)
    columns = lax.all_to_all(first_pair, ("row", "col"), split_axis=1, concat_axis=0, tiled=True)
    normed_cols = layer_norm(columns).astype(jnp.bfloat16)
    projected_cols = jnp.dot(
        normed_cols.reshape(-1, channels), col_project, preferred_element_type=jnp.float32
    ).reshape(length, rows_here, 4 * channels)
    qkv_cols = (
        projected_cols[..., : 3 * channels]
        .astype(jnp.bfloat16)
        .reshape(length, rows_here, 3, head_count, head_size)
    )
    col_ok = tile_rows(local_lines, tile_mask.T, length)
    mixed_cols = attend_lines(
        qkv_cols[:, :, 0],
        qkv_cols[:, :, 1],
        qkv_cols[:, :, 2],
        projected_cols[..., 3 * channels :],
        bias_cols,
        col_ok,
        chain_ids,
        chain_bias[1],
        1,
        True,
    )
    update_cols = jnp.dot(
        mixed_cols.reshape(-1, channels), col_output, preferred_element_type=jnp.float32
    ).reshape(length, rows_here, channels)
    second_pair = (columns.astype(jnp.float32) + update_cols).astype(jnp.bfloat16)
    normed_second = layer_norm(second_pair).astype(jnp.bfloat16)
    edge_mask = tile_pairs(jnp.arange(length, dtype=jnp.int32), local_lines, tile_mask, length)
    left_all = tri_acts(normed_second, tri_left, edge_mask)
    right_all = tri_acts(normed_second, tri_right, edge_mask)
    block_rows = length // n_row
    block_cols = length // n_col

    def one_round(round_index, loop_state):
        product_sum, own_block = loop_state
        left_col = lax.dynamic_index_in_dim(left_all, round_index, 1, keepdims=False)
        right_col = lax.dynamic_index_in_dim(right_all, round_index, 1, keepdims=False)
        raw_col = lax.dynamic_index_in_dim(second_pair, round_index, 1, keepdims=False)
        left_send = jnp.broadcast_to(
            left_col.reshape(n_row, 1, block_rows, channels), (n_row, n_col, block_rows, channels)
        )
        raw_send = jnp.broadcast_to(
            raw_col.reshape(n_row, 1, block_rows, channels), (n_row, n_col, block_rows, channels)
        )
        right_send = jnp.broadcast_to(
            right_col.reshape(1, n_col, block_cols, channels), (n_row, n_col, block_cols, channels)
        )
        outgoing = jnp.concatenate([left_send, raw_send, right_send], axis=2).reshape(
            device_count, 2 * block_rows + block_cols, channels
        )
        received = lax.all_to_all(outgoing, ("row", "col"), split_axis=0, concat_axis=0, tiled=True)
        left_act = received[:, :block_rows].transpose(1, 0, 2)
        right_act = received[:, 2 * block_rows :].transpose(1, 0, 2)
        product_sum = product_sum + jnp.einsum(
            "ikc,jkc->ijc", left_act, right_act, preferred_element_type=jnp.float32
        )
        own_piece = lax.dynamic_slice_in_dim(
            received[:, block_rows : 2 * block_rows], col_index * n_row, n_row, 0
        )
        own_block = lax.dynamic_update_index_in_dim(own_block, own_piece, round_index, 1)
        return (product_sum, own_block)

    initial = (
        jnp.zeros((block_rows, block_cols, channels), jnp.float32),
        jnp.zeros((n_row, rows_here, block_rows, channels), jnp.bfloat16),
    )
    product_sum, own_block = lax.fori_loop(0, rows_here, one_round, initial)
    own_pair = own_block.transpose(2, 0, 1, 3).reshape(block_rows, block_cols, channels)
    normed_own = layer_norm(own_pair).astype(jnp.bfloat16)
    gate_values = jax.nn.sigmoid(
        jnp.dot(normed_own.reshape(-1, channels), tri_gate, preferred_element_type=jnp.float32)
    ).reshape(block_rows, block_cols, channels)
    centered = layer_norm(product_sum).astype(jnp.bfloat16)
    update_tri = jnp.dot(
        centered.reshape(-1, channels), tri_output, preferred_element_type=jnp.float32
    ).reshape(block_rows, block_cols, channels)
    return (own_pair.astype(jnp.float32) + gate_values * update_tri).astype(jnp.bfloat16)


def solution(mesh):
    return jax.shard_map(
        shards,
        mesh=mesh,
        in_specs=(
            P(("row", "col"), None, None),
            P(),
            P(),
            P(),
            P(),
            P(),
            P(),
            P(),
            P(),
            P(),
            P(),
            P(),
            P(),
            P(),
        ),
        out_specs=P("row", "col", None),
        check_vma=False,
    )
```

profile of v0, /device:TPU:1, one launch (start us, length us, event | category | flops | bytes accessed | tf_op | source)
XLA Modules:
  0.0 284.5 jit_solution(12374093587075202309)
XLA Ops:
  0.0 1.1 copy.107
  1.6 0.9 copy-done.1
  3.2 0.6 copy-done.11
  3.9 0.7 copy-done.13
  4.7 66.4 %all_gather.6 = f32[4,128,128]{2,0,1:T(4,128)S(1)} all-gather(f32[4,4,128]{2,0,1:T(4,128)S(1)} %convolution_bitcast_fusion.2), channel_id=1, replica_groups=mesh['row'=8,'col'=4] {'row','col'}, dimensions={1}, use_global_device_ids=true | all-gather | bytes 270336 | tf_op jit(solution)/shard_map/all_gather | solution.py:137
  71.6 0.8 slice-done
  72.5 14.2 %while.42 = (s32[]{:T(128)}, bf16[4,128,128]{1,2,0:T(8,128)(2,1)S(1)}, s32[4]{0:T(128)S(1)}, bf16[4,128,4,32]{1,3,2,0:T(8,128)(2,1)S(1)}, pred[4,128]{1,0:T(4,12...) while((s32[]{:T(128)}, ...), condition=%wide.region_5.6_spmd, body=%wide.region_2.5_spmd.sunk | while | flops 9159427 | bytes 2038731 | solution.py:91
  72.5 0.7 dynamic_slice.179
  76.0 0.7 dynamic_slice.179
  79.6 0.7 dynamic_slice.179
  83.1 0.7 dynamic_slice.179
  86.9 0.8 copy.115
  87.8 0.7 copy-done.14
  88.6 65.4 %all_gather.7 = f32[4,128,128]{2,0,1:T(4,128)S(1)} all-gather(f32[4,4,128]{2,0,1:T(4,128)S(1)} %convolution_bitcast_fusion.1), channel_id=1, replica_groups=mesh['row'=8,'col'=4] {'row','col'}, dimensions={1}, use_global_device_ids=true | all-gather | bytes 270336 | tf_op jit(solution)/shard_map/all_gather | solution.py:168
  154.1 7.7 %all-to-all-start.1 = ((bf16[4,128,128]{2,0,1:T(4,128)(2,1)}), bf16[4,128,128]{2,0,1:T(4,128)(2,1)S(1)}, u32[]{:S(2)}, u32[]{:S(2)}) async-start(bf16[4,128,128]{2,0,1:T(4,128)(2,1)} %copy.115), calls=%async_computation.1 | async-start | bytes 262144 | tf_op jit(solution)/shard_map/all_to_all | solution.py:169
  161.9 7.3 %all-to-all-done.1 = bf16[4,128,128]{2,0,1:T(4,128)(2,1)S(1)} async-done(((bf16[4,128,128]{2,0,1:T(4,128)(2,1)}), bf16[4,128,128]{2,0,1:T(4,128)(2,1)S(1)}, u32[]{:S(2)}, u32[]{:S(2)}) %all-to-all-start.1) | async-done | bytes 131104 | tf_op jit(solution)/shard_map/all_to_all | solution.py:169
  169.4 0.4 multiply_reduce_fusion.2
  169.8 0.3 copy.119
  170.3 0.3 copy.122
  171.1 0.8 copy-done.5
  171.8 0.3 fusion.65
  172.6 13.4 %while.43 = (s32[]{:T(128)}, bf16[4,128,128]{1,2,0:T(8,128)(2,1)S(1)}, s32[4]{0:T(128)S(1)}, bf16[128,4,4,32]{0,3,2,1:T(8,128)(2,1)S(1)}, pred[4,128]{1,0:T(4,12...) while((s32[]{:T(128)}, ...), condition=%wide.region_13.14_spmd, body=%wide.region_10.13_spmd.sunk | while | flops 9159427 | bytes 2038731 | solution.py:91
  172.6 0.6 dynamic_slice.185
  176.0 0.6 dynamic_slice.185
  179.3 0.6 dynamic_slice.185
  182.7 0.6 dynamic_slice.185
  186.4 0.8 copy-done.6
  187.4 0.6 copy-done.7
  188.4 92.2 %while.44 = (s32[]{:T(128)}, f32[16,32,128]{1,0,2:T(8,128)S(1)}, bf16[8,4,16,128]{3,2,0,1:T(8,128)(2,1)S(1)}, bf16[128,4,128]{2,0,1:T(8,128)(2,1)S(1)}, bf16[128...) while((s32[]{:T(128)}, f32[16,32,128]{1,0,2:T(8,128)S(1)}, ...), condition=%wide.region_17.18_spmd.clone, body=%wide.region_16.17_spmd.clone.sunk | while | flops 5898243 | bytes 7373015 | solution.py:236
  188.6 0.5 copy-done.2
  189.2 0.9 pad_maximum_fusion.2
  190.0 3.5 %all-to-all-start = ((bf16[32,64,128]{2,1,0:T(8,128)(2,1)}), bf16[32,64,128]{2,1,0:T(8,128)(2,1)S(1)}, u32[]{:S(2)}, u32[]{:S(2)}) async-start(bf16[32,64,128]{2,1,0:T(8,128)(2,1)} %bitcast.188), calls=%async_computation | async-start | bytes 1048576 | tf_op jit(solution)/shard_map/while/body/eval_jaxpr/all_to_all | solution.py:220
  193.5 15.4 %all-to-all-done = bf16[32,64,128]{2,1,0:T(8,128)(2,1)S(1)} async-done(((bf16[32,64,128]{2,1,0:T(8,128)(2,1)}), bf16[32,64,128]{2,1,0:T(8,128)(2,1)S(1)}, u32[]{:S(2)}, u32[]{:S(2)}) %all-to-all-start) | async-done | bytes 524320 | tf_op jit(solution)/shard_map/while/body/eval_jaxpr/all_to_all | solution.py:220
  208.9 0.5 copy.176
  209.4 1.4 copy.177
  210.9 0.5 fusion.145
  211.4 0.4 copy-done.3
  212.0 0.5 copy-done.2
  212.6 0.9 pad_maximum_fusion.2
  213.4 3.1 %all-to-all-start = ((bf16[32,64,128]{2,1,0:T(8,128)(2,1)}), bf16[32,64,128]{2,1,0:T(8,128)(2,1)S(1)}, u32[]{:S(2)}, u32[]{:S(2)}) async-start(bf16[32,64,128]{2,1,0:T(8,128)(2,1)} %bitcast.188), calls=%async_computation | async-start | bytes 1048576 | tf_op jit(solution)/shard_map/while/body/eval_jaxpr/all_to_all | solution.py:220
  216.6 15.3 %all-to-all-done = bf16[32,64,128]{2,1,0:T(8,128)(2,1)S(1)} async-done(((bf16[32,64,128]{2,1,0:T(8,128)(2,1)}), bf16[32,64,128]{2,1,0:T(8,128)(2,1)S(1)}, u32[]{:S(2)}, u32[]{:S(2)}) %all-to-all-start) | async-done | bytes 524320 | tf_op jit(solution)/shard_map/while/body/eval_jaxpr/all_to_all | solution.py:220
  231.8 0.5 copy.176
  232.3 1.4 copy.177
  233.8 0.5 fusion.145
  234.3 0.4 copy-done.3
  234.9 0.5 copy-done.2
  235.5 0.9 pad_maximum_fusion.2
  236.3 3.2 %all-to-all-start = ((bf16[32,64,128]{2,1,0:T(8,128)(2,1)}), bf16[32,64,128]{2,1,0:T(8,128)(2,1)S(1)}, u32[]{:S(2)}, u32[]{:S(2)}) async-start(bf16[32,64,128]{2,1,0:T(8,128)(2,1)} %bitcast.188), calls=%async_computation | async-start | bytes 1048576 | tf_op jit(solution)/shard_map/while/body/eval_jaxpr/all_to_all | solution.py:220
  239.5 15.3 %all-to-all-done = bf16[32,64,128]{2,1,0:T(8,128)(2,1)S(1)} async-done(((bf16[32,64,128]{2,1,0:T(8,128)(2,1)}), bf16[32,64,128]{2,1,0:T(8,128)(2,1)S(1)}, u32[]{:S(2)}, u32[]{:S(2)}) %all-to-all-start) | async-done | bytes 524320 | tf_op jit(solution)/shard_map/while/body/eval_jaxpr/all_to_all | solution.py:220
  254.8 0.5 copy.176
  255.3 1.4 copy.177
  256.8 0.5 fusion.145
  257.3 0.4 copy-done.3
  257.8 0.5 copy-done.2
  258.4 0.9 pad_maximum_fusion.2
  259.3 3.2 %all-to-all-start = ((bf16[32,64,128]{2,1,0:T(8,128)(2,1)}), bf16[32,64,128]{2,1,0:T(8,128)(2,1)S(1)}, u32[]{:S(2)}, u32[]{:S(2)}) async-start(bf16[32,64,128]{2,1,0:T(8,128)(2,1)} %bitcast.188), calls=%async_computation | async-start | bytes 1048576 | tf_op jit(solution)/shard_map/while/body/eval_jaxpr/all_to_all | solution.py:220
  262.4 15.3 %all-to-all-done = bf16[32,64,128]{2,1,0:T(8,128)(2,1)S(1)} async-done(((bf16[32,64,128]{2,1,0:T(8,128)(2,1)}), bf16[32,64,128]{2,1,0:T(8,128)(2,1)S(1)}, u32[]{:S(2)}, u32[]{:S(2)}) %all-to-all-start) | async-done | bytes 524320 | tf_op jit(solution)/shard_map/while/body/eval_jaxpr/all_to_all | solution.py:220
  277.7 0.5 copy.176
  278.2 1.4 copy.177
  279.7 0.5 fusion.145
  280.2 0.4 copy-done.3
  282.2 0.6 copy-done.12
  283.1 0.4 copy-done.9
  283.6 1.0 fusion.41
  (190 shorter events, 12.9 us)
Async XLA Ops:
  0.0 1.2 copy-start
  1.5 1.0 copy-start.1
  3.2 0.7 copy-start.11
  3.9 0.7 copy-start.13
  71.5 1.0 slice-start
  71.6 0.8 copy-start.4
  72.5 14.2 %copy-start.10 = (bf16[128,128]{1,0:T(8,128)(2,1)S(1)}, bf16[128,128]{1,0:T(8,128)(2,1)}, u32[]{:S(2)}) copy-start(bf16[128,128]{1,0:T(8,128)(2,1)} %param.26) | copy-start | bytes 98308
  87.8 0.7 copy-start.14
  154.1 15.1 %all-to-all-start.1 = ((bf16[4,128,128]{2,0,1:T(4,128)(2,1)}), bf16[4,128,128]{2,0,1:T(4,128)(2,1)S(1)}, u32[]{:S(2)}, u32[]{:S(2)}) async-start(bf16[4,128,128]{2,0,1:T(4,128)(2,1)} %copy.115), calls=%async_computation.1 | async-start | bytes 262144 | tf_op jit(solution)/shard_map/all_to_all | solution.py:169
  170.9 0.9 copy-start.5
  172.6 13.4 %copy-start.8 = (bf16[128,128]{1,0:T(8,128)(2,1)S(1)}, bf16[128,128]{1,0:T(8,128)(2,1)}, u32[]{:S(2)}) copy-start(bf16[128,128]{1,0:T(8,128)(2,1)} %param.29) | copy-start | bytes 98308
  186.3 0.8 copy-start.6
  187.1 0.8 copy-start.7
  188.4 0.7 copy-start.2
  190.0 18.9 %all-to-all-start = ((bf16[32,64,128]{2,1,0:T(8,128)(2,1)}), bf16[32,64,128]{2,1,0:T(8,128)(2,1)S(1)}, u32[]{:S(2)}, u32[]{:S(2)}) async-start(bf16[32,64,128]{2,1,0:T(8,128)(2,1)} %bitcast.188), calls=%async_computation | async-start | bytes 1048576 | tf_op jit(solution)/shard_map/while/body/eval_jaxpr/all_to_all | solution.py:220
  210.9 0.9 copy-start.3
  211.8 0.7 copy-start.2
  213.4 18.4 %all-to-all-start = ((bf16[32,64,128]{2,1,0:T(8,128)(2,1)}), bf16[32,64,128]{2,1,0:T(8,128)(2,1)S(1)}, u32[]{:S(2)}, u32[]{:S(2)}) async-start(bf16[32,64,128]{2,1,0:T(8,128)(2,1)} %bitcast.188), calls=%async_computation | async-start | bytes 1048576 | tf_op jit(solution)/shard_map/while/body/eval_jaxpr/all_to_all | solution.py:220
  233.8 0.9 copy-start.3
  234.7 0.7 copy-start.2
  236.3 18.4 %all-to-all-start = ((bf16[32,64,128]{2,1,0:T(8,128)(2,1)}), bf16[32,64,128]{2,1,0:T(8,128)(2,1)S(1)}, u32[]{:S(2)}, u32[]{:S(2)}) async-start(bf16[32,64,128]{2,1,0:T(8,128)(2,1)} %bitcast.188), calls=%async_computation | async-start | bytes 1048576 | tf_op jit(solution)/shard_map/while/body/eval_jaxpr/all_to_all | solution.py:220
  256.8 0.9 copy-start.3
  257.7 0.7 copy-start.2
  259.3 18.4 %all-to-all-start = ((bf16[32,64,128]{2,1,0:T(8,128)(2,1)}), bf16[32,64,128]{2,1,0:T(8,128)(2,1)S(1)}, u32[]{:S(2)}, u32[]{:S(2)}) async-start(bf16[32,64,128]{2,1,0:T(8,128)(2,1)} %bitcast.188), calls=%async_computation | async-start | bytes 1048576 | tf_op jit(solution)/shard_map/while/body/eval_jaxpr/all_to_all | solution.py:220
  279.7 0.9 copy-start.3
  282.0 0.8 copy-start.12
  282.8 0.8 copy-start.9
where the time goes:
time: 286 us; the launch traced here: 285 us
  blocking collectives  132 us (46%)
  waiting for transfers between devices  68.5 us (24%)
  local copies, waits for them, and re-layouts  29.7 us (10%)
  starting transfers between devices  20.6 us (7%)
  loops' own time  16.9 us (6%)
  matrix products  8.76 us (3%)
  other arithmetic  7.16 us (3%)
    all_gather x1, blocking collectives, shards(): bias_all = lax.all_gather(bias_rows, ('row', 'col'), axis=1, tiled=True)  66.4 us
    all_gather x1, blocking collectives, shards(): bias_cols = lax.all_gather(bias_next, ('row', 'col'), axis=1, tiled=True)  65.4 us
    all_to_all x4, waiting for transfers between devices, one_round(): lax.all_to_all(outgoing, ('row', 'col'), split_axis=0, concat_axis=0, til...  61.2 us
    another operation x2, loops' own time, attend_lines(): lax.map(one_block, jnp.arange(line_count * per_line, dtype=jnp.int32))  16.5 us
    all_to_all x4, starting transfers between devices, one_round(): lax.all_to_all(outgoing, ('row', 'col'), split_axis=0, concat_axis=0, til...  12.9 us
    while x24, local copies, waits for them, and re-layouts  11.2 us
    all_to_all x1, starting transfers between devices, shards(): lax.all_to_all(first_pair, ('row', 'col'), split_axis=1, concat_axis=0, t...  7.68 us
    all_to_all x1, waiting for transfers between devices, shards(): lax.all_to_all(first_pair, ('row', 'col'), split_axis=1, concat_axis=0, t...  7.28 us
  transfers between devices with their start and end apart: 5, of which 5 were waited for; matrix products, arithmetic and copies ran while one was open for 0% of the time, Pallas kernels for 0%

commit v1 on v0

--- a/solution.py
+++ b/solution.py
@@ -2,6 +2,7 @@
 import jax.numpy as jnp
 from jax import lax
 from jax.sharding import PartitionSpec as P
+from jax.lax import all_to_all, axis_size
 
 
 def layer_norm(values):
@@ -165,7 +166,9 @@
         normed_first.reshape(-1, channels), col_bias_proj, preferred_element_type=jnp.float32
     )
     bias_next = bias_next.reshape(rows_here, length, head_count).transpose(2, 0, 1)
-    bias_cols = lax.all_gather(bias_next, ("row", "col"), axis=1, tiled=True)
+    local_out = jnp.stack([bias_next for _ in range(axis_size(("row", "col")))], axis=0)
+    seen_now = all_to_all(local_out, axis_name=("row", "col"), split_axis=0, concat_axis=0)
+    bias_cols = jnp.concatenate(seen_now, 1)
     columns = lax.all_to_all(first_pair, ("row", "col"), split_axis=1, concat_axis=0, tiled=True)
     normed_cols = layer_norm(columns).astype(jnp.bfloat16)
     projected_cols = jnp.dot(

time: 286 us -> 233 us (0.81)
  blocking collectives: 132 us -> 66.4 us
  waiting for transfers between devices: 68.5 us -> 76.2 us
  starting transfers between devices: 20.6 us -> 23.7 us
    all_gather x1 -> x0, blocking collectives: 65.4 us -> none  [shards(): bias_cols = lax.all_gather(bias_next, ('row', 'col'), axis=1, tiled=True)]
    all_to_all x0 -> x1, waiting for transfers between devices: none -> 7.76 us  [shards(): all_to_all(local_out, axis_name=('row', 'col'), split_axis=0, concat_axis=0)]
    all_to_all x0 -> x1, starting transfers between devices: none -> 4.1 us  [shards(): all_to_all(local_out, axis_name=('row', 'col'), split_axis=0, concat_axis=0)]
  transfers between devices with their start and end apart: 5 -> 6, of which waited for: 5 -> 6; matrix products, arithmetic and copies ran while one was open for 0% -> 1% of each run, Pallas kernels for 0% -> 0%
where the time goes in v1:
time: 233 us; the launch traced here: 232 us
  waiting for transfers between devices  76.2 us (33%)
  blocking collectives  66.4 us (28%)
  local copies, waits for them, and re-layouts  31.4 us (13%)
  starting transfers between devices  23.7 us (10%)
  loops' own time  16.9 us (7%)
  matrix products  8.76 us (4%)
  other arithmetic  7.16 us (3%)
    all_gather x1, blocking collectives, shards(): bias_all = lax.all_gather(bias_rows, ('row', 'col'), axis=1, tiled=True)  66.4 us
    all_to_all x4, waiting for transfers between devices, one_round(): lax.all_to_all(outgoing, ('row', 'col'), split_axis=0, concat_axis=0, til...  61 us
    another operation x2, loops' own time, attend_lines(): lax.map(one_block, jnp.arange(line_count * per_line, dtype=jnp.int32))  16.5 us
    all_to_all x4, starting transfers between devices, one_round(): lax.all_to_all(outgoing, ('row', 'col'), split_axis=0, concat_axis=0, til...  12 us
    while x24, local copies, waits for them, and re-layouts  11.2 us
    all_to_all x1, waiting for transfers between devices, shards(): all_to_all(local_out, axis_name=('row', 'col'), split_axis=0, concat_axis=0)  7.76 us
    all_to_all x1, starting transfers between devices, shards(): lax.all_to_all(first_pair, ('row', 'col'), split_axis=1, concat_axis=0, t...  7.6 us
    all_to_all x1, waiting for transfers between devices, shards(): lax.all_to_all(first_pair, ('row', 'col'), split_axis=1, concat_axis=0, t...  7.38 us
  transfers between devices with their start and end apart: 6, of which 6 were waited for; matrix products, arithmetic and copies ran while one was open for 1% of the time, Pallas kernels for 0%

profile of v1, /device:TPU:1, one launch (start us, length us, event | category | flops | bytes accessed | tf_op | source)
XLA Modules:
  0.0 231.7 jit_solution(1387202768305841097)
XLA Ops:
  0.0 1.1 copy.147
  1.6 0.9 copy-done.1
  3.2 0.6 copy-done.11
  3.9 0.7 copy-done.13
  4.7 66.4 %all_gather.3 = f32[4,128,128]{2,0,1:T(4,128)S(1)} all-gather(f32[4,4,128]{2,0,1:T(4,128)S(1)} %convolution_bitcast_fusion.2), channel_id=1, replica_groups=mesh['row'=8,'col'=4] {'row','col'}, dimensions={1}, use_global_device_ids=true | all-gather | bytes 270336 | tf_op jit(solution)/shard_map/all_gather | solution.py:138
  71.6 0.8 slice-done
  72.5 14.2 %while.42 = (s32[]{:T(128)}, bf16[4,128,128]{1,2,0:T(8,128)(2,1)S(1)}, s32[4]{0:T(128)S(1)}, bf16[4,128,4,32]{1,3,2,0:T(8,128)(2,1)S(1)}, pred[4,128]{1,0:T(4,12...) while((s32[]{:T(128)}, ...), condition=%wide.region_5.6_spmd, body=%wide.region_2.5_spmd.sunk | while | flops 9159427 | bytes 2038731 | solution.py:92
  72.5 0.7 dynamic_slice.179
  76.0 0.7 dynamic_slice.179
  79.6 0.7 dynamic_slice.179
  83.1 0.7 dynamic_slice.179
  86.9 0.8 copy.155
  87.8 0.7 copy-done.14
  88.6 7.6 %all-to-all-start.1 = ((bf16[4,128,128]{2,0,1:T(4,128)(2,1)}), bf16[4,128,128]{2,0,1:T(4,128)(2,1)S(1)}, u32[]{:S(2)}, u32[]{:S(2)}) async-start(bf16[4,128,128]{2,0,1:T(4,128)(2,1)} %copy.155), calls=%async_computation.1 | async-start | bytes 262144 | tf_op jit(solution)/shard_map/all_to_all | solution.py:172
  96.4 7.4 %all-to-all-done.1 = bf16[4,128,128]{2,0,1:T(4,128)(2,1)S(1)} async-done(((bf16[4,128,128]{2,0,1:T(4,128)(2,1)}), bf16[4,128,128]{2,0,1:T(4,128)(2,1)S(1)}, u32[]{:S(2)}, u32[]{:S(2)}) %all-to-all-start.1) | async-done | bytes 131104 | tf_op jit(solution)/shard_map/all_to_all | solution.py:172
  104.0 0.4 multiply_reduce_fusion.2
  104.4 0.7 stack.2
  105.1 4.1 %all-to-all-start.2 = ((f32[32,4,4,128]{3,2,1,0:T(4,128)}), f32[32,4,4,128]{3,2,1,0:T(4,128)}, u32[]{:S(2)}, u32[]{:S(2)}) async-start(f32[32,4,4,128]{3,2,1,0:T(4,128)} %stack.2), calls=%async_computation.2 | async-start | bytes 524288 | tf_op jit(solution)/shard_map/all_to_all | solution.py:170
  110.5 0.8 copy-done.5
  112.0 7.8 %all-to-all-done.2 = f32[32,4,4,128]{3,2,1,0:T(4,128)} async-done(((f32[32,4,4,128]{3,2,1,0:T(4,128)}), f32[32,4,4,128]{3,2,1,0:T(4,128)}, u32[]{:S(2)}, u32[]{:S(2)}) %all-to-all-start.2) | async-done | bytes 262176 | tf_op jit(solution)/shard_map/all_to_all | solution.py:170
  119.8 1.0 copy.166
  120.8 13.4 %while.43 = (s32[]{:T(128)}, bf16[4,128,128]{1,2,0:T(8,128)(2,1)S(1)}, s32[4]{0:T(128)S(1)}, bf16[128,4,4,32]{0,3,2,1:T(8,128)(2,1)S(1)}, pred[4,128]{1,0:T(4,12...) while((s32[]{:T(128)}, ...), condition=%wide.region_13.14_spmd, body=%wide.region_10.13_spmd.sunk | while | flops 9159427 | bytes 2038731 | solution.py:92
  120.8 0.6 dynamic_slice.185
  124.2 0.6 dynamic_slice.185
  127.5 0.6 dynamic_slice.185
  130.9 0.6 dynamic_slice.185
  134.6 0.8 copy-done.6
  135.6 0.6 copy-done.7
  136.6 91.2 %while.44 = (s32[]{:T(128)}, f32[16,32,128]{1,0,2:T(8,128)S(1)}, bf16[8,4,16,128]{3,2,0,1:T(8,128)(2,1)S(1)}, bf16[128,4,128]{2,0,1:T(8,128)(2,1)S(1)}, bf16[128...) while((s32[]{:T(128)}, f32[16,32,128]{1,0,2:T(8,128)S(1)}, ...), condition=%wide.region_17.18_spmd.clone, body=%wide.region_16.17_spmd.clone.sunk | while | flops 5898243 | bytes 7373015 | solution.py:239
  136.8 0.5 copy-done.2
  137.4 0.9 pad_maximum_fusion.2
  138.2 2.5 %all-to-all-start = ((bf16[32,64,128]{2,1,0:T(8,128)(2,1)}), bf16[32,64,128]{2,1,0:T(8,128)(2,1)S(1)}, u32[]{:S(2)}, u32[]{:S(2)}) async-start(bf16[32,64,128]{2,1,0:T(8,128)(2,1)} %bitcast.190), calls=%async_computation | async-start | bytes 1048576 | tf_op jit(solution)/shard_map/while/body/eval_jaxpr/all_to_all | solution.py:223
  140.8 15.3 %all-to-all-done = bf16[32,64,128]{2,1,0:T(8,128)(2,1)S(1)} async-done(((bf16[32,64,128]{2,1,0:T(8,128)(2,1)}), bf16[32,64,128]{2,1,0:T(8,128)(2,1)S(1)}, u32[]{:S(2)}, u32[]{:S(2)}) %all-to-all-start) | async-done | bytes 524320 | tf_op jit(solution)/shard_map/while/body/eval_jaxpr/all_to_all | solution.py:223
  156.0 0.5 copy.217
  156.6 1.4 copy.218
  158.0 0.5 fusion.145
  158.6 0.4 copy-done.3
  159.1 0.5 copy-done.2
  159.7 0.9 pad_maximum_fusion.2
  160.5 3.1 %all-to-all-start = ((bf16[32,64,128]{2,1,0:T(8,128)(2,1)}), bf16[32,64,128]{2,1,0:T(8,128)(2,1)S(1)}, u32[]{:S(2)}, u32[]{:S(2)}) async-start(bf16[32,64,128]{2,1,0:T(8,128)(2,1)} %bitcast.190), calls=%async_computation | async-start | bytes 1048576 | tf_op jit(solution)/shard_map/while/body/eval_jaxpr/all_to_all | solution.py:223
  163.7 15.3 %all-to-all-done = bf16[32,64,128]{2,1,0:T(8,128)(2,1)S(1)} async-done(((bf16[32,64,128]{2,1,0:T(8,128)(2,1)}), bf16[32,64,128]{2,1,0:T(8,128)(2,1)S(1)}, u32[]{:S(2)}, u32[]{:S(2)}) %all-to-all-start) | async-done | bytes 524320 | tf_op jit(solution)/shard_map/while/body/eval_jaxpr/all_to_all | solution.py:223
  179.0 0.5 copy.217
  179.5 1.4 copy.218
  181.0 0.5 fusion.145
  181.5 0.4 copy-done.3
  182.0 0.5 copy-done.2
  182.6 0.9 pad_maximum_fusion.2
  183.5 3.2 %all-to-all-start = ((bf16[32,64,128]{2,1,0:T(8,128)(2,1)}), bf16[32,64,128]{2,1,0:T(8,128)(2,1)S(1)}, u32[]{:S(2)}, u32[]{:S(2)}) async-start(bf16[32,64,128]{2,1,0:T(8,128)(2,1)} %bitcast.190), calls=%async_computation | async-start | bytes 1048576 | tf_op jit(solution)/shard_map/while/body/eval_jaxpr/all_to_all | solution.py:223
  186.6 15.3 %all-to-all-done = bf16[32,64,128]{2,1,0:T(8,128)(2,1)S(1)} async-done(((bf16[32,64,128]{2,1,0:T(8,128)(2,1)}), bf16[32,64,128]{2,1,0:T(8,128)(2,1)S(1)}, u32[]{:S(2)}, u32[]{:S(2)}) %all-to-all-start) | async-done | bytes 524320 | tf_op jit(solution)/shard_map/while/body/eval_jaxpr/all_to_all | solution.py:223
  201.9 0.5 copy.217
  202.4 1.4 copy.218
  203.9 0.5 fusion.145
  204.4 0.4 copy-done.3
  205.0 0.5 copy-done.2
  205.6 0.9 pad_maximum_fusion.2
  206.4 3.2 %all-to-all-start = ((bf16[32,64,128]{2,1,0:T(8,128)(2,1)}), bf16[32,64,128]{2,1,0:T(8,128)(2,1)S(1)}, u32[]{:S(2)}, u32[]{:S(2)}) async-start(bf16[32,64,128]{2,1,0:T(8,128)(2,1)} %bitcast.190), calls=%async_computation | async-start | bytes 1048576 | tf_op jit(solution)/shard_map/while/body/eval_jaxpr/all_to_all | solution.py:223
  209.6 15.3 %all-to-all-done = bf16[32,64,128]{2,1,0:T(8,128)(2,1)S(1)} async-done(((bf16[32,64,128]{2,1,0:T(8,128)(2,1)}), bf16[32,64,128]{2,1,0:T(8,128)(2,1)S(1)}, u32[]{:S(2)}, u32[]{:S(2)}) %all-to-all-start) | async-done | bytes 524320 | tf_op jit(solution)/shard_map/while/body/eval_jaxpr/all_to_all | solution.py:223
  224.9 0.5 copy.217
  225.4 1.4 copy.218
  226.9 0.5 fusion.145
  227.4 0.4 copy-done.3
  229.4 0.6 copy-done.12
  230.3 0.4 copy-done.9
  230.7 1.0 fusion.41
  (193 shorter events, 13.9 us)
Async XLA Ops:
  0.0 1.2 copy-start
  1.5 1.0 copy-start.1
  3.2 0.7 copy-start.11
  3.9 0.7 copy-start.13
  71.5 1.0 slice-start
  71.6 0.8 copy-start.4
  72.5 14.2 %copy-start.10 = (bf16[128,128]{1,0:T(8,128)(2,1)S(1)}, bf16[128,128]{1,0:T(8,128)(2,1)}, u32[]{:S(2)}) copy-start(bf16[128,128]{1,0:T(8,128)(2,1)} %param.26) | copy-start | bytes 98308
  87.8 0.7 copy-start.14
  88.6 15.1 %all-to-all-start.1 = ((bf16[4,128,128]{2,0,1:T(4,128)(2,1)}), bf16[4,128,128]{2,0,1:T(4,128)(2,1)S(1)}, u32[]{:S(2)}, u32[]{:S(2)}) async-start(bf16[4,128,128]{2,0,1:T(4,128)(2,1)} %copy.155), calls=%async_computation.1 | async-start | bytes 262144 | tf_op jit(solution)/shard_map/all_to_all | solution.py:172
  105.1 14.6 %all-to-all-start.2 = ((f32[32,4,4,128]{3,2,1,0:T(4,128)}), f32[32,4,4,128]{3,2,1,0:T(4,128)}, u32[]{:S(2)}, u32[]{:S(2)}) async-start(f32[32,4,4,128]{3,2,1,0:T(4,128)} %stack.2), calls=%async_computation.2 | async-start | bytes 524288 | tf_op jit(solution)/shard_map/all_to_all | solution.py:170
  110.4 0.9 copy-start.5
  120.8 13.4 %copy-start.8 = (bf16[128,128]{1,0:T(8,128)(2,1)S(1)}, bf16[128,128]{1,0:T(8,128)(2,1)}, u32[]{:S(2)}) copy-start(bf16[128,128]{1,0:T(8,128)(2,1)} %param.29) | copy-start | bytes 98308
  134.5 0.8 copy-start.6
  135.3 0.8 copy-start.7
  136.6 0.7 copy-start.2
  138.2 17.8 %all-to-all-start = ((bf16[32,64,128]{2,1,0:T(8,128)(2,1)}), bf16[32,64,128]{2,1,0:T(8,128)(2,1)S(1)}, u32[]{:S(2)}, u32[]{:S(2)}) async-start(bf16[32,64,128]{2,1,0:T(8,128)(2,1)} %bitcast.190), calls=%async_computation | async-start | bytes 1048576 | tf_op jit(solution)/shard_map/while/body/eval_jaxpr/all_to_all | solution.py:223
  158.0 0.9 copy-start.3
  158.9 0.7 copy-start.2
  160.5 18.4 %all-to-all-start = ((bf16[32,64,128]{2,1,0:T(8,128)(2,1)}), bf16[32,64,128]{2,1,0:T(8,128)(2,1)S(1)}, u32[]{:S(2)}, u32[]{:S(2)}) async-start(bf16[32,64,128]{2,1,0:T(8,128)(2,1)} %bitcast.190), calls=%async_computation | async-start | bytes 1048576 | tf_op jit(solution)/shard_map/while/body/eval_jaxpr/all_to_all | solution.py:223
  181.0 0.9 copy-start.3
  181.9 0.7 copy-start.2
  183.5 18.4 %all-to-all-start = ((bf16[32,64,128]{2,1,0:T(8,128)(2,1)}), bf16[32,64,128]{2,1,0:T(8,128)(2,1)S(1)}, u32[]{:S(2)}, u32[]{:S(2)}) async-start(bf16[32,64,128]{2,1,0:T(8,128)(2,1)} %bitcast.190), calls=%async_computation | async-start | bytes 1048576 | tf_op jit(solution)/shard_map/while/body/eval_jaxpr/all_to_all | solution.py:223
  203.9 0.9 copy-start.3
  204.8 0.7 copy-start.2
  206.4 18.4 %all-to-all-start = ((bf16[32,64,128]{2,1,0:T(8,128)(2,1)}), bf16[32,64,128]{2,1,0:T(8,128)(2,1)S(1)}, u32[]{:S(2)}, u32[]{:S(2)}) async-start(bf16[32,64,128]{2,1,0:T(8,128)(2,1)} %bitcast.190), calls=%async_computation | async-start | bytes 1048576 | tf_op jit(solution)/shard_map/while/body/eval_jaxpr/all_to_all | solution.py:223
  226.8 0.9 copy-start.3
  229.2 0.8 copy-start.12
  229.9 0.8 copy-start.9
